TPU v7x, 32 devices: a whole 2x2x4 slice. The times are simulated.
32 devices in a mesh: rep: 4 (over y, core), seq: 4 (over z), fsdp: 2 (over x).
Axes of the slice: x: 2, y: 2, z: 4, core: 2. Of those that a mesh axis runs over, the one named last changes fastest.
Arguments:
- tokens: bfloat16 [4096, 4096], P(('rep', 'seq')), may hold values from -6 to 6
- cotangent: bfloat16 [4096, 4096], P(('rep', 'seq')), may hold values from -3 to 3
- norm_gain: float32 [4096], replicated, may hold values from 0.1 to 1.9
- gate_weight: bfloat16 [4096, 12288], P(None, ('seq', 'fsdp')), may hold values from -0.09375 to 0.09375
- up_weight: bfloat16 [4096, 12288], P(None, ('seq', 'fsdp')), may hold values from -0.09375 to 0.09375
- down_weight: bfloat16 [12288, 4096], P(('seq', 'fsdp')), may hold values from -0.0546875 to 0.0546875
- depths: int32 [4096], P(('rep', 'seq')), may hold values from 0 to 4, as said below
Outputs:
- branch_grad: bfloat16 [4096, 4096], P(('rep', 'seq', 'fsdp'))
- gate_grad: float32 [4096, 12288], P('rep', ('seq', 'fsdp'))
- up_grad: float32 [4096, 12288], P('rep', ('seq', 'fsdp'))
- down_grad: float32 [12288, 4096], P(('seq', 'fsdp'), 'rep')
Inputs may be any that keep to these rules, and one draw needn't show every extreme that they name: `depths`: within each aligned block of 256 rows (the tokens of one seq shard) at most 8 and at least 4 tokens have a depth greater than 1, and some block has exactly 8.
All inputs are finite; a program needn't handle non-finite values.
Results may differ from a plain program's by a relative error of at most 0.019.
Values may be sent and summed in bfloat16 or wider, within the bound.
No kernel may reach another device: no remote copies, remote signals or barrier semaphores. Data moves between devices by JAX's collectives and lax.ppermute only.
A program may use at most 192 MiB of HBM per device.

v0:
```python
from functools import partial
import jax
import jax.numpy as jnp
from jax import lax
from jax.sharding import PartitionSpec as P

REC = 1
MAXACT = 8
EPSILON = 1e-05


def normalize(widened, norm_gain):
    factor = lax.rsqrt(jnp.mean(widened * widened, axis=-1, keepdims=True) + EPSILON)
    return widened * factor * norm_gain


def contract_first(left, right):
    return lax.dot_general(
        left, right, (((0,), (0,)), ((), ())), preferred_element_type=jnp.float32
    )


def contract_last(left, right):
    return lax.dot_general(
        left, right, (((1,), (1,)), ((), ())), preferred_element_type=jnp.float32
    )


def local(tokens, cotangent, norm_gain, gate_weight, up_weight, down_weight, depths):
    parts = lax.axis_size("fsdp")
    place = lax.axis_index("fsdp")
    replicas = lax.axis_size("rep")
    replica = lax.axis_index("rep")
    features = tokens.shape[1]
    feature_share = features // replicas
    rows_here = tokens.shape[0]
    own_rows = rows_here // parts
    active = depths > REC
    ordinal = jnp.cumsum(active.astype(jnp.int32)) - 1
    selector = (ordinal[None, :] == jnp.arange(MAXACT, dtype=jnp.int32)[:, None]) & active[None, :]
    picker = selector.astype(jnp.bfloat16)
    source = jnp.dot(picker, tokens, preferred_element_type=jnp.float32)
    send_masked = jnp.dot(picker, cotangent, preferred_element_type=jnp.float32).astype(
        jnp.bfloat16
    )
    send_normed = normalize(source, norm_gain).astype(jnp.bfloat16)
    all_normed = lax.all_gather(send_normed, ("rep", "seq"), axis=0, tiled=True)
    all_masked = lax.all_gather(send_masked, ("rep", "seq"), axis=0, tiled=True)
    gate = jnp.dot(all_normed, gate_weight, preferred_element_type=jnp.float32)
    up = jnp.dot(all_normed, up_weight, preferred_element_type=jnp.float32)
    sigmoid_gate = jax.nn.sigmoid(gate)
    swished = gate * sigmoid_gate
    hidden = (swished * up).astype(jnp.bfloat16)
    hidden_grad = contract_last(all_masked, down_weight)
    gate_rows = (hidden_grad * up * sigmoid_gate * (1.0 + gate * (1.0 - sigmoid_gate))).astype(
        jnp.bfloat16
    )
    up_rows = (hidden_grad * swished).astype(jnp.bfloat16)
    normed_cols = lax.dynamic_slice_in_dim(all_normed, replica * feature_share, feature_share, 1)
    masked_cols = lax.dynamic_slice_in_dim(all_masked, replica * feature_share, feature_share, 1)
    gate_grad = contract_first(normed_cols, gate_rows)
    up_grad = contract_first(normed_cols, up_rows)
    down_grad = contract_first(hidden, masked_cols)
    window = all_normed.shape[0] // replicas
    window_gate = lax.dynamic_slice_in_dim(gate_rows, replica * window, window, 0)
    window_up = lax.dynamic_slice_in_dim(up_rows, replica * window, window, 0)
    partial_features = contract_last(window_gate, gate_weight) + contract_last(window_up, up_weight)
    slot_count = send_normed.shape[0]
    share = slot_count // parts
    feature_grad = lax.psum_scatter(
        partial_features.astype(jnp.bfloat16), ("seq", "fsdp"), scatter_dimension=0, tiled=True
    ).astype(jnp.float32)
    mine = lax.dynamic_slice_in_dim(source, place * share, share, 0)
    _, pullback = jax.vjp(partial(normalize, norm_gain=norm_gain), mine)
    slot_grad = pullback(feature_grad)[0].astype(jnp.bfloat16)
    every_slot = lax.all_gather(slot_grad, "fsdp", axis=0, tiled=True)
    own_columns = lax.dynamic_slice_in_dim(picker, place * own_rows, own_rows, 1)
    branch_grad = contract_first(own_columns, every_slot).astype(jnp.bfloat16)
    return (branch_grad, gate_grad, up_grad, down_grad)


def solution(mesh):
    in_specs = (
        P(("rep", "seq"), None),
        P(("rep", "seq"), None),
        P(),
        P(None, ("seq", "fsdp")),
        P(None, ("seq", "fsdp")),
        P(("seq", "fsdp"), None),
        P(("rep", "seq")),
    )
    out_specs = (
        P(("rep", "seq", "fsdp"), None),
        P("rep", ("seq", "fsdp")),
        P("rep", ("seq", "fsdp")),
        P(("seq", "fsdp"), "rep"),
    )
    return jax.shard_map(local, mesh=mesh, in_specs=in_specs, out_specs=out_specs, check_vma=False)
```

profile of v0, /device:TPU:0, one launch (start us, length us, event | category | flops | bytes accessed | tf_op | source)
XLA Modules:
  0.0 198.2 jit_solution(12777274194914511911)
XLA Ops:
  7.2 0.0 copy-start
  7.2 0.0 all-gather.6.cloned.1.call-start
  7.2 0.8 convert_bitcast_fusion
  8.1 0.3 reduce-window.9
  8.4 0.1 slice.7
  8.5 0.1 slice_reduce_fusion
  8.6 0.1 add_bitcast_fusion
  8.7 0.1 copy-done
  8.8 0.5 multiply_reduce_fusion
  9.3 1.4 multiply_convert_fusion.4
  10.7 0.0 all-gather.6.cloned.1.call-update
  10.7 0.0 all-gather.4.cloned.1.call-start
  10.8 2.6 %convolution_convert_fusion.1 = bf16[8,4096]{1,0:T(8,128)(2,1)} fusion(bf16[256,4096]{1,0:T(8,128)(2,1)} %param.8, s32[256]{0:T(256)S(1)} %add_bitcast_fusion, pred[256]{0:T(512)(128)(4,1)S(1)} %get-tuple-element.7), kind=kOutput, calls=%fused_computation.3 | convolution fusion | flops 16814080 | bytes 2163968 | tf_op jit(solution)/shard_map/dot_general | solution.py:43
  13.4 0.0 all-gather.4.cloned.1.call-update
  13.4 0.0 all-reduce.3.cloned.1.call-start
  13.5 1.2 dynamic-slice
  15.4 36.2 %all-gather.6.cloned.1.call-done = bf16[128,4096]{1,0:T(8,128)(2,1)} async-done(((bf16[8,4096]{1,0:T(8,128)(2,1)}), bf16[128,4096]{1,0:T(8,128)(2,1)}) %all-gather.6.cloned.1.call-update) | async-done | bytes 1048592 | tf_op jit(solution)/shard_map/all_gather | solution.py:47
  51.6 6.8 %fusion.28 = f32[128,1536]{1,0:T(8,128)S(1)} fusion(bf16[128,4096]{1,0:T(8,128)(2,1)} %all-gather.6.cloned.1.call-done, bf16[4096,1536]{1,0:T(8,128)(2,1)} %param.10), kind=kOutput, calls=%fused_computation.46 | convolution fusion | flops 1610612736 | bytes 14417920 | tf_op jit(solution)/shard_map/dot_general | solution.py:49
  58.4 6.7 %fusion.27 = f32[128,1536]{1,0:T(8,128)S(1)} fusion(bf16[128,4096]{1,0:T(8,128)(2,1)S(1)} %copy-done.2, bf16[4096,1536]{1,0:T(8,128)(2,1)} %param.11), kind=kOutput, calls=%fused_computation.45 | convolution fusion | flops 1610612736 | bytes 14417920 | tf_op jit(solution)/shard_map/dot_general | solution.py:50
  65.1 26.1 %all-gather.4.cloned.1.call-done = bf16[128,4096]{1,0:T(8,128)(2,1)} async-done(((bf16[8,4096]{1,0:T(8,128)(2,1)}), bf16[128,4096]{1,0:T(8,128)(2,1)}) %all-gather.4.cloned.1.call-update) | async-done | bytes 1048592 | tf_op jit(solution)/shard_map/all_gather | solution.py:48
  91.3 9.4 %multiply_convert_fusion.1 = (bf16[128,1536]{1,0:T(8,128)(2,1)S(1)}, bf16[128,1536]{1,0:T(8,128)(2,1)S(1)}) fusion(f32[128,1536]{1,0:T(8,128)S(1)} %fusion.28, f32[128,1536]{1,0:T(8,128)S(1)} %fusion.27, bf16[128,4096]{1,0:T(8,128)(2,1)} %all-gather.4.cloned.1.call-done, bf16[1536,4096]{1,0:T(8,128)(2,1)} %param.12), kind=kOutput, calls=%fused_computation.5 | convolution fusion | flops 1613168640 | bytes 15990784 | tf_op jit(solution)/shard_map/dot_general | solution.py:24
  100.8 8.6 %fusion.10 = f32[32,4096]{1,0:T(8,128)S(1)} fusion(bf16[4096,1536]{1,0:T(8,128)(2,1)} %param.10, bf16[128,1536]{1,0:T(8,128)(2,1)S(1)} %get-tuple-element.9, s32[]{:T(128)S(6)} %select_n.15), kind=kOutput, calls=%fused_computation.19 | convolution fusion | flops 402653184 | bytes 13205508 | tf_op jit(solution)/shard_map/dot_general | solution.py:24
  109.4 4.5 %fusion = bf16[32,4096]{1,0:T(8,128)(2,1)} fusion(f32[32,4096]{1,0:T(8,128)S(1)} %fusion.10, bf16[4096,1536]{1,0:T(8,128)(2,1)S(1)} %bitcast.21, bf16[128,1536]{1,0:T(8,128)(2,1)S(1)} %get-tuple-element.8, s32[]{:T(128)S(6)} %select_n.15), kind=kOutput, calls=%fused_computation.2 | convolution fusion | flops 402915328 | bytes 13467652 | tf_op jit(solution)/shard_map/dot_general | solution.py:24
  113.9 0.0 all-reduce.3.cloned.1.call-update
  114.0 5.3 %fusion.2 = f32[1536,1024]{1,0:T(8,128)} fusion(f32[128,1536]{1,0:T(8,128)} %copy-done.4, bf16[128,4096]{1,0:T(8,128)(2,1)} %all-gather.4.cloned.1.call-done, s32[]{:T(128)S(6)} %select_n.17, f32[128,1536]{1,0:T(8,128)} %copy-done.3), kind=kOutput, calls=%fused_computation.9 | convolution fusion | flops 403832832 | bytes 8126468 | tf_op jit(solution)/shard_map/dot_general | solution.py:18
  119.3 3.7 %fusion.4 = f32[1024,1536]{1,0:T(8,128)} fusion(bf16[128,1536]{1,0:T(8,128)(2,1)S(1)} %copy-done.8, bf16[128,4096]{1,0:T(8,128)(2,1)S(1)} %copy-done.2, s32[]{:T(128)S(6)} %select_n.17), kind=kOutput, calls=%fused_computation.11 | convolution fusion | flops 402653184 | bytes 6946820 | tf_op jit(solution)/shard_map/dot_general | solution.py:18
  123.0 3.7 %fusion.6 = f32[1024,1536]{1,0:T(8,128)} fusion(bf16[128,1536]{1,0:T(8,128)(2,1)S(1)} %copy-done.6, bf16[128,4096]{1,0:T(8,128)(2,1)S(1)} %copy-done.2, s32[]{:T(128)S(6)} %select_n.17), kind=kOutput, calls=%fused_computation.13 | convolution fusion | flops 402653184 | bytes 6946820 | tf_op jit(solution)/shard_map/dot_general | solution.py:18
  126.7 56.8 %all-reduce.3.cloned.1.call-done = bf16[32,4096]{1,0:T(8,128)(2,1)} async-done(((bf16[32,4096]{1,0:T(8,128)(2,1)}), bf16[32,4096]{1,0:T(8,128)(2,1)}) %all-reduce.3.cloned.1.call-update) | async-done | bytes 262160
  183.6 1.0 multiply_reduce_fusion.2
  184.6 0.9 fusion.13
  185.6 4.6 %all-gather = bf16[2,4,4096]{2,1,0:T(4,128)(2,1)S(1)} all-gather(bf16[1,4,4096]{2,1,0:T(4,128)(2,1)S(1)} %fusion.13), channel_id=1, replica_groups=mesh['rep'=4,'seq'=4,'fsdp'=2] {'fsdp'}, dimensions={0}, use_global_device_ids=true | all-gather | bytes 98304 | tf_op jit(solution)/shard_map/all_gather | solution.py:76
  190.2 1.5 convolution_convert_fusion
  (30 shorter events, 0.2 us)
Async XLA Ops:
  7.2 1.6 copy-start
  7.2 44.4 %all-gather.6.cloned.1.call-start = ((), (), s32[]{:S(2)}) async-start(), calls=%async_computation.1 | async-start | bytes 1114112 | tf_op jit(solution)/shard_map/all_gather | solution.py:47
  10.7 80.5 %all-gather.4.cloned.1.call-start = ((), (), s32[]{:S(2)}) async-start(), calls=%async_computation | async-start | bytes 1114112 | tf_op jit(solution)/shard_map/all_gather | solution.py:48
  13.4 170.2 %all-reduce.3.cloned.1.call-start = ((), (), s32[]{:S(2)}) async-start(), calls=%async_computation.2 | async-start | bytes 524288
  51.6 6.8 %copy-start.2 = (bf16[128,4096]{1,0:T(8,128)(2,1)S(1)}, bf16[128,4096]{1,0:T(8,128)(2,1)}, u32[]{:S(2)}) copy-start(bf16[128,4096]{1,0:T(8,128)(2,1)} %all-gather.6.cloned.1.call-done) | copy-start | bytes 3145732
  58.4 42.3 %copy-start.3 = (f32[128,1536]{1,0:T(8,128)}, f32[128,1536]{1,0:T(8,128)S(1)}, u32[]{:S(2)}) copy-start(f32[128,1536]{1,0:T(8,128)S(1)} %fusion.28) | copy-start | bytes 2359300
  65.1 44.2 %copy-start.4 = (f32[128,1536]{1,0:T(8,128)}, f32[128,1536]{1,0:T(8,128)S(1)}, u32[]{:S(2)}) copy-start(f32[128,1536]{1,0:T(8,128)S(1)} %fusion.27) | copy-start | bytes 2359300
  91.3 18.1 %slice-start = ((s8[12582912]{0:T(1024)(128)(4,1)}), s8[4194304]{0:T(1024)(128)(4,1)S(1)}, s32[]{:S(2)}) async-start(s8[12582912]{0:T(1024)(128)(4,1)} %bitcast.20), calls=%async_computation.3 | async-start | bytes 8388608
  91.3 18.2 %slice-start.1 = ((s8[12582912]{0:T(1024)(128)(4,1)}), s8[4194304]{0:T(1024)(128)(4,1)S(1)}, s32[]{:S(2)}) async-start(s8[12582912]{0:T(1024)(128)(4,1)} %bitcast.20), calls=%async_computation.4 | async-start | bytes 8388608
  100.7 8.7 %copy-start.5 = (bf16[128,1536]{1,0:T(8,128)(2,1)}, bf16[128,1536]{1,0:T(8,128)(2,1)S(1)}, u32[]{:S(2)}) copy-start(bf16[128,1536]{1,0:T(8,128)(2,1)S(1)} %get-tuple-element.9) | copy-start | bytes 1179652
  100.7 8.7 %copy-start.7 = (bf16[128,1536]{1,0:T(8,128)(2,1)}, bf16[128,1536]{1,0:T(8,128)(2,1)S(1)}, u32[]{:S(2)}) copy-start(bf16[128,1536]{1,0:T(8,128)(2,1)S(1)} %get-tuple-element.8) | copy-start | bytes 1179652
  100.7 8.7 %slice-start.2 = ((s8[12582912]{0:T(1024)(128)(4,1)}), s8[4194304]{0:T(1024)(128)(4,1)S(1)}, s32[]{:S(2)}) async-start(s8[12582912]{0:T(1024)(128)(4,1)} %bitcast.20), calls=%async_computation.5 | async-start | bytes 8388608
  113.9 5.4 %copy-start.8 = (bf16[128,1536]{1,0:T(8,128)(2,1)S(1)}, bf16[128,1536]{1,0:T(8,128)(2,1)}, u32[]{:S(2)}) copy-start(bf16[128,1536]{1,0:T(8,128)(2,1)} %copy-done.7) | copy-start | bytes 1179652
  113.9 9.1 %copy-start.6 = (bf16[128,1536]{1,0:T(8,128)(2,1)S(1)}, bf16[128,1536]{1,0:T(8,128)(2,1)}, u32[]{:S(2)}) copy-start(bf16[128,1536]{1,0:T(8,128)(2,1)} %copy-done.5) | copy-start | bytes 1179652
  114.0 77.7 %copy-start.1 = (bf16[256,4096]{1,0:T(8,128)(2,1)S(1)}, bf16[256,4096]{1,0:T(8,128)(2,1)}, u32[]{:S(2)}) copy-start(bf16[256,4096]{1,0:T(8,128)(2,1)} %param.7) | copy-start | bytes 6291460
  119.3 64.3 %copy-start.9 = (f32[4096]{0:T(1024)S(1)}, f32[4096]{0:T(1024)}, u32[]{:S(2)}) copy-start(f32[4096]{0:T(1024)} %param.9) | copy-start | bytes 49156
Sparse Core Ops, SparseCore 0:
  10.9 40.6 all-gather.5
  54.4 36.8 all-gather.3
  114.1 69.4 all-reduce.2
where the time goes:
time: 199 us; the launch traced here: 198 us
  waiting for transfers between devices  119 us (60%)
  matrix products  53.4 us (27%)
  between operations  14.6 us (7%)
  other arithmetic  4.69 us (2%)
  blocking collectives  4.59 us (2%)
    unnamed x4, waiting for transfers between devices  56.9 us
    all_gather x1, waiting for transfers between devices, local(): all_normed = lax.all_gather(send_normed, ('rep', 'seq'), axis=0, tiled=True)  36.2 us
    all_gather x1, waiting for transfers between devices, local(): all_masked = lax.all_gather(send_masked, ('rep', 'seq'), axis=0, tiled=True)  26.1 us
    dot_general x3, matrix products, contract_last(): lax.dot_general(left, right, (((1,), (1,)), ((), ())), preferred_element_...  22.5 us
    dot_general x4, matrix products, contract_first(): lax.dot_general(left, right, (((0,), (0,)), ((), ())), preferred_element_...  14.2 us
    dot_general x1, matrix products, local(): gate = jnp.dot(all_normed, gate_weight, preferred_element_type=jnp.float32)  6.77 us
    dot_general x1, matrix products, local(): up = jnp.dot(all_normed, up_weight, preferred_element_type=jnp.float32)  6.74 us
    all_gather x1, blocking collectives, local(): every_slot = lax.all_gather(slot_grad, 'fsdp', axis=0, tiled=True)  4.59 us
  transfers between devices with their start and end apart: 3, of which 3 were waited for; matrix products, arithmetic and copies ran while one was open for 15% of the time, Pallas kernels for 0%

commit v1 on v0

--- a/solution.py
+++ b/solution.py
@@ -44,8 +44,13 @@
         jnp.bfloat16
     )
     send_normed = normalize(source, norm_gain).astype(jnp.bfloat16)
-    all_normed = lax.all_gather(send_normed, ("rep", "seq"), axis=0, tiled=True)
-    all_masked = lax.all_gather(send_masked, ("rep", "seq"), axis=0, tiled=True)
+    all_normed, all_masked = jnp.split(
+        lax.all_gather(
+            jnp.concatenate([send_normed, send_masked], axis=1), ("rep", "seq"), axis=0, tiled=True
+        ),
+        [send_normed.shape[1]],
+        axis=1,
+    )
     gate = jnp.dot(all_normed, gate_weight, preferred_element_type=jnp.float32)
     up = jnp.dot(all_normed, up_weight, preferred_element_type=jnp.float32)
     sigmoid_gate = jax.nn.sigmoid(gate)

time: 199 us -> 180 us (0.905)
  waiting for transfers between devices: 119 us -> 99.3 us
    all_gather x2 -> x1, waiting for transfers between devices: 62.3 us -> 42.3 us  [local(): lax.all_gather(jnp.concatenate([send_normed, send_masked], axis=1), ('rep...]
    unnamed x4 -> x3, waiting for transfers between devices: 56.9 us -> 57 us
  transfers between devices with their start and end apart: 3 -> 2, of which waited for: 3 -> 2; matrix products, arithmetic and copies ran while one was open for 15% -> 8% of each run, Pallas kernels for 0% -> 0%
where the time goes in v1:
time: 180 us; the launch traced here: 179 us
  waiting for transfers between devices  99.3 us (55%)
  matrix products  53.1 us (30%)
  between operations  14.8 us (8%)
  other arithmetic  4.73 us (3%)
  blocking collectives  4.59 us (3%)
  local copies, waits for them, and re-layouts  2.51 us (1%)
    unnamed x3, waiting for transfers between devices  57 us
    all_gather x1, waiting for transfers between devices, local(): lax.all_gather(jnp.concatenate([send_normed, send_masked], axis=1), ('rep...  42.3 us
    dot_general x3, matrix products, contract_last(): lax.dot_general(left, right, (((1,), (1,)), ((), ())), preferred_element_...  23.6 us
    dot_general x4, matrix products, contract_first(): lax.dot_general(left, right, (((0,), (0,)), ((), ())), preferred_element_...  13.8 us
    dot_general x1, matrix products, local(): gate = jnp.dot(all_normed, gate_weight, preferred_element_type=jnp.float32)  6.83 us
    dot_general x1, matrix products, local(): up = jnp.dot(all_normed, up_weight, preferred_element_type=jnp.float32)  6.37 us
    all_gather x1, blocking collectives, local(): every_slot = lax.all_gather(slot_grad, 'fsdp', axis=0, tiled=True)  4.59 us
  transfers between devices with their start and end apart: 2, of which 2 were waited for; matrix products, arithmetic and copies ran while one was open for 8% of the time, Pallas kernels for 0%

profile of v1, /device:TPU:0, one launch (start us, length us, event | category | flops | bytes accessed | tf_op | source)
XLA Modules:
  0.0 179.1 jit_solution(371037297371422239)
XLA Ops:
  7.2 0.0 copy-start
  7.2 0.0 all-gather.3.cloned.1.call-start
  7.2 0.8 convert_bitcast_fusion
  8.1 0.3 reduce-window.9
  8.4 0.1 slice.7
  8.5 0.1 slice_reduce_fusion
  8.6 0.1 add_bitcast_fusion
  8.7 2.0 %convolution_convert_fusion.1 = bf16[8,4096]{1,0:T(8,128)(2,1)S(1)} fusion(bf16[256,4096]{1,0:T(8,128)(2,1)} %param.8, s32[256]{0:T(256)S(1)} %add_bitcast_fusion, pred[256]{0:T(512)(128)(4,1)S(1)} %get-tuple-element.7), kind=kOutput, calls=%fused_computation.3 | convolution fusion | flops 16814080 | bytes 2163968 | tf_op jit(solution)/shard_map/dot_general | solution.py:43
  10.6 0.5 multiply_reduce_fusion
  11.2 0.8 multiply_convert_fusion.4
  12.0 0.7 pad_maximum_fusion
  12.6 0.0 all-gather.3.cloned.1.call-update
  12.7 0.0 all-reduce.3.cloned.1.call-start
  12.7 1.2 dynamic-slice
  14.6 42.3 %all-gather.3.cloned.1.call-done = bf16[128,8192]{1,0:T(8,128)(2,1)} async-done(((bf16[8,8192]{1,0:T(8,128)(2,1)}), bf16[128,8192]{1,0:T(8,128)(2,1)}) %all-gather.3.cloned.1.call-update) | async-done | bytes 2097168 | tf_op jit(solution)/shard_map/all_gather | solution.py:48
  56.9 6.8 %fusion.29 = f32[128,1536]{1,0:T(8,128)S(1)} fusion(bf16[4096,1536]{1,0:T(8,128)(2,1)} %param.10, bf16[128,8192]{1,0:T(8,128)(2,1)} %all-gather.3.cloned.1.call-done), kind=kOutput, calls=%fused_computation.48 | convolution fusion | flops 1610612736 | bytes 14417920 | tf_op jit(solution)/shard_map/dot_general | solution.py:54
  63.8 6.4 %fusion.31 = f32[128,1536]{1,0:T(8,128)S(1)} fusion(bf16[4096,1536]{1,0:T(8,128)(2,1)} %param.11, bf16[128,8192]{1,0:T(8,128)(2,1)S(1)} %copy-done.2), kind=kOutput, calls=%fused_computation.50 | convolution fusion | flops 1610612736 | bytes 14417920 | tf_op jit(solution)/shard_map/dot_general | solution.py:55
  70.2 0.9 copy-done.3
  71.0 9.8 %multiply_convert_fusion.1 = (bf16[128,1536]{1,0:T(8,128)(2,1)}, bf16[128,1536]{1,0:T(8,128)(2,1)S(1)}) fusion(f32[128,1536]{1,0:T(8,128)S(1)} %fusion.29, f32[128,1536]{1,0:T(8,128)S(1)} %fusion.31, bf16[1536,4096]{1,0:T(8,128)(2,1)} %param.12, bf16[128,8192]{1,0:T(8,128)(2,1)S(1)} %copy-done.2), kind=kOutput, calls=%fused_computation.5 | convolution fusion | flops 1613168640 | bytes 15990784 | tf_op jit(solution)/shard_map/dot_general | solution.py:24
  80.9 8.4 %fusion.10 = f32[32,4096]{1,0:T(8,128)S(1)} fusion(bf16[4096,1536]{1,0:T(8,128)(2,1)} %param.10, bf16[128,1536]{1,0:T(8,128)(2,1)S(1)} %get-tuple-element.11, s32[]{:T(128)S(6)} %select_n.15), kind=kOutput, calls=%fused_computation.20 | convolution fusion | flops 402653184 | bytes 13205508 | tf_op jit(solution)/shard_map/dot_general | solution.py:24
  89.3 0.0 slice-done.1
  89.4 5.3 %fusion = bf16[32,4096]{1,0:T(8,128)(2,1)} fusion(f32[32,4096]{1,0:T(8,128)S(1)} %fusion.10, bf16[4096,1536]{1,0:T(8,128)(2,1)S(1)} %bitcast.18, bf16[128,1536]{1,0:T(8,128)(2,1)} %get-tuple-element.10, s32[]{:T(128)S(6)} %select_n.15), kind=kOutput, calls=%fused_computation.2 | convolution fusion | flops 402915328 | bytes 13467652 | tf_op jit(solution)/shard_map/dot_general | solution.py:24
  94.7 0.0 all-reduce.3.cloned.1.call-update
  94.7 0.1 fusion.33
  94.9 4.9 %fusion.2 = f32[1536,1024]{1,0:T(8,128)} fusion(f32[128,1536]{1,0:T(8,128)} %copy-done.3, bf16[128,4096]{1,0:T(8,128)(2,1)S(1)} %get-tuple-element.8, s32[]{:T(128)S(6)} %select_n.17, f32[128,1536]{1,0:T(8,128)S(1)} %fusion.29), kind=kOutput, calls=%fused_computation.9 | convolution fusion | flops 403832832 | bytes 8126468 | tf_op jit(solution)/shard_map/dot_general | solution.py:18
  99.8 3.7 %fusion.4 = f32[1024,1536]{1,0:T(8,128)} fusion(bf16[128,1536]{1,0:T(8,128)(2,1)S(1)} %copy-done.4, bf16[128,4096]{1,0:T(8,128)(2,1)S(1)} %get-tuple-element.9, s32[]{:T(128)S(6)} %select_n.17), kind=kOutput, calls=%fused_computation.11 | convolution fusion | flops 402653184 | bytes 6946820 | tf_op jit(solution)/shard_map/dot_general | solution.py:18
  103.5 3.7 %fusion.6 = f32[1024,1536]{1,0:T(8,128)} fusion(bf16[128,1536]{1,0:T(8,128)(2,1)S(1)} %get-tuple-element.11, bf16[128,4096]{1,0:T(8,128)(2,1)S(1)} %get-tuple-element.9, s32[]{:T(128)S(6)} %select_n.17), kind=kOutput, calls=%fused_computation.13 | convolution fusion | flops 402653184 | bytes 6946820 | tf_op jit(solution)/shard_map/dot_general | solution.py:18
  107.2 57.0 %all-reduce.3.cloned.1.call-done = bf16[32,4096]{1,0:T(8,128)(2,1)} async-done(((bf16[32,4096]{1,0:T(8,128)(2,1)}), bf16[32,4096]{1,0:T(8,128)(2,1)}) %all-reduce.3.cloned.1.call-update) | async-done | bytes 262160
  164.2 1.0 multiply_reduce_fusion.2
  165.3 0.9 fusion.13
  166.2 4.6 %all-gather = bf16[2,4,4096]{2,1,0:T(4,128)(2,1)S(1)} all-gather(bf16[1,4,4096]{2,1,0:T(4,128)(2,1)S(1)} %fusion.13), channel_id=1, replica_groups=mesh['rep'=4,'seq'=4,'fsdp'=2] {'fsdp'}, dimensions={0}, use_global_device_ids=true | all-gather | bytes 98304 | tf_op jit(solution)/shard_map/all_gather | solution.py:81
  170.8 1.5 convolution_convert_fusion
  (21 shorter events, 0.1 us)
Async XLA Ops:
  7.2 3.5 %copy-start = (bf16[256,4096]{1,0:T(8,128)(2,1)S(1)}, bf16[256,4096]{1,0:T(8,128)(2,1)}, u32[]{:S(2)}) copy-start(bf16[256,4096]{1,0:T(8,128)(2,1)} %param.7) | copy-start | bytes 6291460
  7.2 49.7 %all-gather.3.cloned.1.call-start = ((), (), s32[]{:S(2)}) async-start(), calls=%async_computation | async-start | bytes 2228224 | tf_op jit(solution)/shard_map/all_gather | solution.py:48
  12.7 151.5 %all-reduce.3.cloned.1.call-start = ((), (), s32[]{:S(2)}) async-start(), calls=%async_computation.1 | async-start | bytes 524288
  56.9 6.8 %copy-start.2 = (bf16[128,8192]{1,0:T(8,128)(2,1)S(1)}, bf16[128,8192]{1,0:T(8,128)(2,1)}, u32[]{:S(2)}) copy-start(bf16[128,8192]{1,0:T(8,128)(2,1)} %all-gather.3.cloned.1.call-done) | copy-start | bytes 6291460
  70.1 0.9 copy-start.3
  71.0 18.3 %slice-start = ((s8[12582912]{0:T(1024)(128)(4,1)}), s8[4194304]{0:T(1024)(128)(4,1)S(1)}, s32[]{:S(2)}) async-start(s8[12582912]{0:T(1024)(128)(4,1)} %bitcast.17), calls=%async_computation.2 | async-start | bytes 8388608
  71.0 18.3 %slice-start.1 = ((s8[12582912]{0:T(1024)(128)(4,1)}), s8[4194304]{0:T(1024)(128)(4,1)S(1)}, s32[]{:S(2)}) async-start(s8[12582912]{0:T(1024)(128)(4,1)} %bitcast.17), calls=%async_computation.3 | async-start | bytes 8388608
  80.9 8.5 %slice-start.2 = ((s8[12582912]{0:T(1024)(128)(4,1)}), s8[4194304]{0:T(1024)(128)(4,1)S(1)}, s32[]{:S(2)}) async-start(s8[12582912]{0:T(1024)(128)(4,1)} %bitcast.17), calls=%async_computation.4 | async-start | bytes 8388608
  94.9 4.9 %copy-start.4 = (bf16[128,1536]{1,0:T(8,128)(2,1)S(1)}, bf16[128,1536]{1,0:T(8,128)(2,1)}, u32[]{:S(2)}) copy-start(bf16[128,1536]{1,0:T(8,128)(2,1)} %get-tuple-element.10) | copy-start | bytes 1179652
  99.8 72.5 %copy-start.1 = (bf16[256,4096]{1,0:T(8,128)(2,1)S(1)}, bf16[256,4096]{1,0:T(8,128)(2,1)}, u32[]{:S(2)}) copy-start(bf16[256,4096]{1,0:T(8,128)(2,1)} %param.7) | copy-start | bytes 6291460
  103.5 60.7 %copy-start.5 = (f32[4096]{0:T(1024)S(1)}, f32[4096]{0:T(1024)}, u32[]{:S(2)}) copy-start(f32[4096]{0:T(1024)} %param.9) | copy-start | bytes 49156
Sparse Core Ops, SparseCore 0:
  12.8 44.0 all-gather.2
  94.9 69.3 all-reduce.2
